TPU v7x, 512 devices: a whole 4x4x16 slice. The times are simulated.
512 devices in a mesh: section: 8 (over y, core), dp: 64 (over x, z).
Axes of the slice: x: 4, y: 4, z: 16, core: 2. Of those that a mesh axis runs over, the one named last changes fastest.
Arguments:
- queries: bfloat16 [8, 8192, 2560], P('section', 'dp')
- key_cells: bfloat16 [8, 8192, 2560], P('section', 'dp')
- value_cells: bfloat16 [8, 8192, 2560], P('section', 'dp'), may hold values from -6 to 6
- grad_cells: bfloat16 [8, 8192, 2560], P('section', 'dp'), may hold values from -6 to 6
- packing: int32 [8, 64, 128], P('section', 'dp'), may hold values from 0 to 127, each once within a row
- segment_ids: int32 [8, 8192], P('section'), may hold values from 0 to 511, never falling along the last dimension, each value on 1 to 32 neighbouring positions
Outputs:
- input_grads: bfloat16 [8, 8192, 7680], P('section', 'dp')
Inputs may be any that keep to these rules, and one draw needn't show every extreme that they name: `packing`: each row of a section and device is a permutation of 0 to 127. `segment_ids`: along a section's packed cells the ids never fall; each segment has 1 to 32 cells and one has exactly 32.
All inputs are finite; a program needn't handle non-finite values.
Results may differ from a plain program's by a relative error of at most 0.0086.
Values may be sent and summed in bfloat16 or wider, within the bound.
No kernel may reach another device: no remote copies, remote signals or barrier semaphores. Data moves between devices by JAX's collectives and lax.ppermute only.
A program may use at most 64 MiB of HBM per device.

v0:
```python
import jax
import jax.numpy as jnp
from jax import lax
from jax.sharding import PartitionSpec as P

HEADS = 20
HEAD_DIM = 128


def with_halo(value, sides, width):
    for axis, dim in sides:
        size, length = (lax.axis_size(axis), value.shape[dim])
        up = [(i, (i + 1) % size) for i in range(size - 1)]
        down = [(j, i) for i, j in up]
        last = lax.slice_in_dim(value, length - width, length, axis=dim)
        initial = lax.slice_in_dim(value, 0, width, axis=dim)
        before = lax.ppermute(last, axis, up)
        after = lax.ppermute(initial, axis, down)
        value = jnp.concatenate([before, value, after], axis=dim)
    return value


def passed_along(value, axis, steps):
    count = lax.axis_size(axis)
    initial, last = (max(0, -steps), min(count, count - steps))
    return lax.ppermute(value, axis, [(source, source + steps) for source in range(initial, last)])


def from_behind(block, axis, distance):
    devices = range(lax.axis_size(axis))
    route = [((i - distance) % len(devices), i) for i in devices]
    return lax.ppermute(block, axis, route)


def heads_of(matrix):
    return matrix.reshape(matrix.shape[0], HEADS, HEAD_DIM)


def masked_scores(query_rows, key_rows, query_ids, key_ids):
    scores = jnp.einsum(
        "ihd,jhd->hij", heads_of(query_rows), heads_of(key_rows), preferred_element_type=jnp.float32
    )
    scores = scores * HEAD_DIM ** (-0.5)
    allowed = (query_ids[:, None] == key_ids[None, :])[None]
    return jnp.where(allowed, scores, -jnp.inf)


def body(queries, key_cells, value_cells, grad_cells, packing, segment_ids):
    cell_count = queries.shape[1]
    width = queries.shape[2]
    groups = lax.axis_size("dp")
    per_peer = cell_count // groups
    reach = cell_count // 4
    place = lax.axis_index("dp")
    scale = HEAD_DIM ** (-0.5)
    order = packing[0, 0]

    def pack(matrix):
        return matrix[0][order].reshape(groups, per_peer, width)

    arrived = (
        lax.all_to_all(pack(queries), "dp", split_axis=0, concat_axis=0, tiled=True),
        lax.all_to_all(pack(key_cells), "dp", split_axis=0, concat_axis=0, tiled=True),
        lax.all_to_all(pack(value_cells), "dp", split_axis=0, concat_axis=0, tiled=True),
        lax.all_to_all(pack(grad_cells), "dp", split_axis=0, concat_axis=0, tiled=True),
    )
    own_q, own_k, own_v, own_g = [piece.reshape(cell_count, width) for piece in arrived]
    rim_ids = jnp.full((reach,), -1, jnp.int32)
    padded_ids = jnp.concatenate([rim_ids, segment_ids[0], rim_ids])
    window_ids = lax.dynamic_slice_in_dim(padded_ids, place * cell_count, cell_count + 2 * reach)
    own_ids = window_ids[reach : reach + cell_count]
    key_value = jnp.concatenate([own_k, own_v], axis=1)
    key_value_window = with_halo(key_value, (("dp", 0),), reach)
    key_window = key_value_window[:, :width]
    value_window = key_value_window[:, width:]
    scores = masked_scores(own_q, key_window, own_ids, window_ids)
    top = jnp.max(scores, axis=2)
    log_total = top + jnp.log(jnp.sum(jnp.exp(scores - top[:, :, None]), axis=2))
    probs = jnp.exp(scores - log_total[:, :, None])
    probs_low = probs.astype(jnp.bfloat16)
    grad_heads = heads_of(own_g)
    attended = jnp.einsum(
        "hij,jhd->ihd", probs_low, heads_of(value_window), preferred_element_type=jnp.float32
    )
    delta = jnp.sum(grad_heads.astype(jnp.float32) * attended, axis=2).T
    dprobs = jnp.einsum(
        "ihd,jhd->hij", grad_heads, heads_of(value_window), preferred_element_type=jnp.float32
    )
    dscores = (probs * (dprobs - delta[:, :, None]) * scale).astype(jnp.bfloat16)
    grad_query = jnp.einsum(
        "hij,jhd->ihd", dscores, heads_of(key_window), preferred_element_type=jnp.float32
    )
    grad_query = grad_query.reshape(cell_count, width).astype(jnp.bfloat16)
    window = cell_count + 2 * reach
    grad_key = jnp.einsum(
        "hij,ihd->jhd", dscores, heads_of(own_q), preferred_element_type=jnp.float32
    )
    grad_value = jnp.einsum(
        "hij,ihd->jhd", probs_low, grad_heads, preferred_element_type=jnp.float32
    )
    partial_value = jnp.concatenate(
        [grad_key.reshape(window, width), grad_value.reshape(window, width)], axis=1
    )
    from_after = passed_along(partial_value[:reach].astype(jnp.bfloat16), "dp", -1).astype(
        jnp.float32
    )
    from_before = passed_along(
        partial_value[reach + cell_count :].astype(jnp.bfloat16), "dp", 1
    ).astype(jnp.float32)
    summed = partial_value[reach : reach + cell_count]
    summed = summed.at[cell_count - reach :].add(from_after)
    summed = summed.at[:reach].add(from_before)
    packed_grads = jnp.concatenate([grad_query, summed.astype(jnp.bfloat16)], axis=1)
    returned = lax.all_to_all(
        packed_grads.reshape(groups, per_peer, 3 * width),
        "dp",
        split_axis=0,
        concat_axis=0,
        tiled=True,
    )
    returned = returned.reshape(cell_count, 3 * width)
    inverse = (
        jnp.zeros((cell_count,), jnp.int32).at[order].set(jnp.arange(cell_count, dtype=jnp.int32))
    )
    loaded_order = returned[inverse]
    handed = from_behind(loaded_order, "section", -1)
    return handed[None]


def solution(mesh):
    return jax.shard_map(
        body,
        mesh=mesh,
        in_specs=(
            P("section", "dp", None),
            P("section", "dp", None),
            P("section", "dp", None),
            P("section", "dp", None),
            P("section", "dp", None),
            P("section", None),
        ),
        out_specs=P("section", "dp", None),
        check_vma=False,
    )
```

profile of v0, /device:TPU:1, one launch (start us, length us, event | category | flops | bytes accessed | tf_op | source)
XLA Modules:
  0.0 359.2 jit_solution(15673436810725732558)
XLA Ops:
  3.2 19.1 %all-to-all-start.3 = ((bf16[64,2,2560]{2,1,0:T(2,128)(2,1)}), bf16[64,2,2560]{2,1,0:T(2,128)(2,1)S(1)}, u32[]{:S(2)}, u32[]{:S(2)}) async-start(bf16[64,2,2560]{2,1,0:T(2,128)(2,1)} %reshape.158), calls=%async_computation.3 | async-start | bytes 1310720 | tf_op jit(solution)/shard_map/all_to_all | solution.py:65
  24.4 32.3 %all-to-all-done.3 = bf16[64,2,2560]{2,1,0:T(2,128)(2,1)S(1)} async-done(((bf16[64,2,2560]{2,1,0:T(2,128)(2,1)}), bf16[64,2,2560]{2,1,0:T(2,128)(2,1)S(1)}, u32[]{:S(2)}, u32[]{:S(2)}) %all-to-all-start.3) | async-done | bytes 655392 | tf_op jit(solution)/shard_map/all_to_all | solution.py:65
  56.7 9.2 %all-to-all-start.1 = ((bf16[64,2,2560]{2,1,0:T(2,128)(2,1)}), bf16[64,2,2560]{2,1,0:T(2,128)(2,1)S(1)}, u32[]{:S(2)}, u32[]{:S(2)}) async-start(bf16[64,2,2560]{2,1,0:T(2,128)(2,1)} %reshape.154), calls=%async_computation.1 | async-start | bytes 1310720 | tf_op jit(solution)/shard_map/all_to_all | solution.py:64
  68.0 32.2 %all-to-all-done.1 = bf16[64,2,2560]{2,1,0:T(2,128)(2,1)S(1)} async-done(((bf16[64,2,2560]{2,1,0:T(2,128)(2,1)}), bf16[64,2,2560]{2,1,0:T(2,128)(2,1)S(1)}, u32[]{:S(2)}, u32[]{:S(2)}) %all-to-all-start.1) | async-done | bytes 655392 | tf_op jit(solution)/shard_map/all_to_all | solution.py:64
  100.2 9.5 %all-to-all-start = ((bf16[64,2,2560]{2,1,0:T(2,128)(2,1)}), bf16[64,2,2560]{2,1,0:T(2,128)(2,1)}, u32[]{:S(2)}, u32[]{:S(2)}) async-start(bf16[64,2,2560]{2,1,0:T(2,128)(2,1)} %reshape.152), calls=%async_computation | async-start | bytes 1310720 | tf_op jit(solution)/shard_map/all_to_all | solution.py:63
  111.8 32.1 %all-to-all-done = bf16[64,2,2560]{2,1,0:T(2,128)(2,1)} async-done(((bf16[64,2,2560]{2,1,0:T(2,128)(2,1)}), bf16[64,2,2560]{2,1,0:T(2,128)(2,1)}, u32[]{:S(2)}, u32[]{:S(2)}) %all-to-all-start) | async-done | bytes 655392 | tf_op jit(solution)/shard_map/all_to_all | solution.py:63
  143.9 9.5 %all-to-all-start.2 = ((bf16[64,2,2560]{2,1,0:T(2,128)(2,1)}), bf16[64,2,2560]{2,1,0:T(2,128)(2,1)}, u32[]{:S(2)}, u32[]{:S(2)}) async-start(bf16[64,2,2560]{2,1,0:T(2,128)(2,1)} %reshape.157), calls=%async_computation.2 | async-start | bytes 1310720 | tf_op jit(solution)/shard_map/all_to_all | solution.py:62
  153.6 2.7 reshape.153
  158.5 3.6 collective-permute-start
  162.0 1.5 collective-permute-start.1
  164.8 22.5 %all-to-all-done.2 = bf16[64,2,2560]{2,1,0:T(2,128)(2,1)} async-done(((bf16[64,2,2560]{2,1,0:T(2,128)(2,1)}), bf16[64,2,2560]{2,1,0:T(2,128)(2,1)}, u32[]{:S(2)}, u32[]{:S(2)}) %all-to-all-start.2) | async-done | bytes 655392 | tf_op jit(solution)/shard_map/all_to_all | solution.py:62
  187.3 2.2 reshape_reshape.7
  195.9 1.3 collective-permute-start.2
  197.4 1.4 convolution_convert_fusion
  198.8 2.2 copy.20
  201.0 5.4 %collective-permute-start.3 = (bf16[32,5120]{1,0:T(8,128)(2,1)}, bf16[32,5120]{1,0:T(8,128)(2,1)S(1)}, u32[]{:S(2)}, u32[]{:S(2)}) collective-permute-start(bf16[32,5120]{1,0:T(8,128)(2,1)} %get-tuple-element.29), channel_id=1, source_target_pairs={{0,1},{1,2},{2,3},{3,4},{4,5},{5,6},{6,7},{7,8},{8,9},{9,10},{10,1... | collective-permute-start | bytes 983048 | tf_op jit(solution)/shard_map/ppermute | solution.py:26
  207.7 3.1 collective-permute-done.3
  212.1 1.7 reshape.162
  213.8 19.4 %all-to-all-start.4 = ((bf16[64,2,7680]{2,1,0:T(2,128)(2,1)}), bf16[64,2,7680]{2,1,0:T(2,128)(2,1)}, u32[]{:S(2)}, u32[]{:S(2)}) async-start(bf16[64,2,7680]{2,1,0:T(2,128)(2,1)} %reshape.162), calls=%async_computation.4 | async-start | bytes 3932160 | tf_op jit(solution)/shard_map/all_to_all | solution.py:114
  234.3 84.8 %all-to-all-done.4 = bf16[64,2,7680]{2,1,0:T(2,128)(2,1)} async-done(((bf16[64,2,7680]{2,1,0:T(2,128)(2,1)}), bf16[64,2,7680]{2,1,0:T(2,128)(2,1)}, u32[]{:S(2)}, u32[]{:S(2)}) %all-to-all-start.4) | async-done | bytes 1966112 | tf_op jit(solution)/shard_map/all_to_all | solution.py:114
  319.1 4.2 %reshape.163 = bf16[128,7680]{1,0:T(8,128)(2,1)S(1)} reshape(bf16[64,2,7680]{2,1,0:T(2,128)(2,1)} %all-to-all-done.4) | data formatting | bytes 3932160 | tf_op jit(solution)/shard_map/reshape | solution.py:121
  323.3 3.1 gather_fusion.4
  326.4 7.8 %collective-permute-start.4 = (bf16[128,7680]{1,0:T(8,128)(2,1)}, bf16[128,7680]{1,0:T(8,128)(2,1)S(1)}, u32[]{:S(2)}, u32[]{:S(2)}) collective-permute-start(bf16[128,7680]{1,0:T(8,128)(2,1)} %gather_fusion.4), channel_id=1, source_target_pairs={{64,0},{128,64},{192,128},{256,192},{320,256},{384,320},{448,384},... | collective-permute-start | bytes 5898248 | tf_op jit(solution)/shard_map/ppermute | solution.py:32
  334.2 23.7 %collective-permute-done.4 = bf16[128,7680]{1,0:T(8,128)(2,1)S(1)} collective-permute-done((bf16[128,7680]{1,0:T(8,128)(2,1)}, bf16[128,7680]{1,0:T(8,128)(2,1)S(1)}, u32[]{:S(2)}, u32[]{:S(2)}) %collective-permute-start.4) | collective-permute-done | bytes 1966112 | tf_op jit(solution)/shard_map/ppermute | solution.py:32
  (61 shorter events, 24.3 us)
Async XLA Ops:
  0.0 1.1 copy-start
  2.1 20.2 %copy-start.1 = (bf16[1,128,2560]{2,1,0:T(8,128)(2,1)S(1)}, bf16[1,128,2560]{2,1,0:T(8,128)(2,1)}, u32[]{:S(2)}) copy-start(bf16[1,128,2560]{2,1,0:T(8,128)(2,1)} %param.12) | copy-start | bytes 1966084
  3.2 53.5 %all-to-all-start.3 = ((bf16[64,2,2560]{2,1,0:T(2,128)(2,1)}), bf16[64,2,2560]{2,1,0:T(2,128)(2,1)S(1)}, u32[]{:S(2)}, u32[]{:S(2)}) async-start(bf16[64,2,2560]{2,1,0:T(2,128)(2,1)} %reshape.158), calls=%async_computation.3 | async-start | bytes 1310720 | tf_op jit(solution)/shard_map/all_to_all | solution.py:65
  23.3 42.7 %copy-start.2 = (bf16[1,128,2560]{2,1,0:T(8,128)(2,1)S(1)}, bf16[1,128,2560]{2,1,0:T(8,128)(2,1)}, u32[]{:S(2)}) copy-start(bf16[1,128,2560]{2,1,0:T(8,128)(2,1)} %param.11) | copy-start | bytes 1966084
  56.7 43.5 %all-to-all-start.1 = ((bf16[64,2,2560]{2,1,0:T(2,128)(2,1)}), bf16[64,2,2560]{2,1,0:T(2,128)(2,1)S(1)}, u32[]{:S(2)}, u32[]{:S(2)}) async-start(bf16[64,2,2560]{2,1,0:T(2,128)(2,1)} %reshape.154), calls=%async_computation.1 | async-start | bytes 1310720 | tf_op jit(solution)/shard_map/all_to_all | solution.py:64
  66.9 42.8 %copy-start.3 = (bf16[1,128,2560]{2,1,0:T(8,128)(2,1)S(1)}, bf16[1,128,2560]{2,1,0:T(8,128)(2,1)}, u32[]{:S(2)}) copy-start(bf16[1,128,2560]{2,1,0:T(8,128)(2,1)} %param.10) | copy-start | bytes 1966084
  100.2 43.7 %all-to-all-start = ((bf16[64,2,2560]{2,1,0:T(2,128)(2,1)}), bf16[64,2,2560]{2,1,0:T(2,128)(2,1)}, u32[]{:S(2)}, u32[]{:S(2)}) async-start(bf16[64,2,2560]{2,1,0:T(2,128)(2,1)} %reshape.152), calls=%async_computation | async-start | bytes 1310720 | tf_op jit(solution)/shard_map/all_to_all | solution.py:63
  143.9 43.4 %all-to-all-start.2 = ((bf16[64,2,2560]{2,1,0:T(2,128)(2,1)}), bf16[64,2,2560]{2,1,0:T(2,128)(2,1)}, u32[]{:S(2)}, u32[]{:S(2)}) async-start(bf16[64,2,2560]{2,1,0:T(2,128)(2,1)} %reshape.157), calls=%async_computation.2 | async-start | bytes 1310720 | tf_op jit(solution)/shard_map/all_to_all | solution.py:62
  156.4 7.2 %copy-start.6 = (s32[1,8192]{1,0:T(1,128)S(1)}, s32[1,8192]{1,0:T(1,128)}, u32[]{:S(2)}) copy-start(s32[1,8192]{1,0:T(1,128)} %param.15) | copy-start | bytes 98308
  158.5 31.0 %collective-permute-start = (bf16[32,5120]{1,0:T(8,128)(2,1)}, bf16[32,5120]{1,0:T(8,128)(2,1)}, u32[]{:S(2)}, u32[]{:S(2)}) collective-permute-start(bf16[32,5120]{1,0:T(8,128)(2,1)} %get-tuple-element.33), channel_id=1, source_target_pairs={{0,1},{1,2},{2,3},{3,4},{4,5},{5,6},{6,7},{7,8},{8,9},{9,10},{10,1... | collective-permute-start | bytes 983048 | tf_op jit(solution)/shard_map/ppermute | solution.py:17
  162.0 27.5 %collective-permute-start.1 = (bf16[32,5120]{1,0:T(8,128)(2,1)}, bf16[32,5120]{1,0:T(8,128)(2,1)}, u32[]{:S(2)}, u32[]{:S(2)}) collective-permute-start(bf16[32,5120]{1,0:T(8,128)(2,1)} %get-tuple-element.34), channel_id=1, source_target_pairs={{1,0},{2,1},{3,2},{4,3},{5,4},{6,5},{7,6},{8,7},{9,8},{10,9},{11,1... | collective-permute-start | bytes 983048 | tf_op jit(solution)/shard_map/ppermute | solution.py:18
  194.5 2.7 copy-start.4
  195.9 10.5 %collective-permute-start.2 = (bf16[32,5120]{1,0:T(8,128)(2,1)}, bf16[32,5120]{1,0:T(8,128)(2,1)}, u32[]{:S(2)}, u32[]{:S(2)}) collective-permute-start(bf16[32,5120]{1,0:T(8,128)(2,1)} %get-tuple-element.30), channel_id=1, source_target_pairs={{1,0},{2,1},{3,2},{4,3},{5,4},{6,5},{7,6},{8,7},{9,8},{10,9},{11,1... | collective-permute-start | bytes 983048 | tf_op jit(solution)/shard_map/ppermute | solution.py:26
  201.0 9.8 %collective-permute-start.3 = (bf16[32,5120]{1,0:T(8,128)(2,1)}, bf16[32,5120]{1,0:T(8,128)(2,1)S(1)}, u32[]{:S(2)}, u32[]{:S(2)}) collective-permute-start(bf16[32,5120]{1,0:T(8,128)(2,1)} %get-tuple-element.29), channel_id=1, source_target_pairs={{0,1},{1,2},{2,3},{3,4},{4,5},{5,6},{6,7},{7,8},{8,9},{9,10},{10,1... | collective-permute-start | bytes 983048 | tf_op jit(solution)/shard_map/ppermute | solution.py:26
  210.9 1.1 copy-start.5
  213.8 105.3 %all-to-all-start.4 = ((bf16[64,2,7680]{2,1,0:T(2,128)(2,1)}), bf16[64,2,7680]{2,1,0:T(2,128)(2,1)}, u32[]{:S(2)}, u32[]{:S(2)}) async-start(bf16[64,2,7680]{2,1,0:T(2,128)(2,1)} %reshape.162), calls=%async_computation.4 | async-start | bytes 3932160 | tf_op jit(solution)/shard_map/all_to_all | solution.py:114
  326.4 31.5 %collective-permute-start.4 = (bf16[128,7680]{1,0:T(8,128)(2,1)}, bf16[128,7680]{1,0:T(8,128)(2,1)S(1)}, u32[]{:S(2)}, u32[]{:S(2)}) collective-permute-start(bf16[128,7680]{1,0:T(8,128)(2,1)} %gather_fusion.4), channel_id=1, source_target_pairs={{64,0},{128,64},{192,128},{256,192},{320,256},{384,320},{448,384},... | collective-permute-start | bytes 5898248 | tf_op jit(solution)/shard_map/ppermute | solution.py:32
where the time goes:
time: 360 us; the launch traced here: 359 us
  waiting for transfers between devices  231 us (64%)
  starting transfers between devices  86.4 us (24%)
  local copies, waits for them, and re-layouts  33.3 us (9%)
  matrix products  4.32 us (1%)
  other arithmetic  4.21 us (1%)
    all_to_all x1, waiting for transfers between devices, body(): lax.all_to_all(packed_grads.reshape(groups, per_peer, 3 * width), 'dp', s...  84.8 us
    all_to_all x1, waiting for transfers between devices, body(): lax.all_to_all(pack(grad_cells), 'dp', split_axis=0, concat_axis=0, tiled...  32.3 us
    all_to_all x1, waiting for transfers between devices, body(): lax.all_to_all(pack(value_cells), 'dp', split_axis=0, concat_axis=0, tile...  32.2 us
    all_to_all x1, waiting for transfers between devices, body(): lax.all_to_all(pack(key_cells), 'dp', split_axis=0, concat_axis=0, tiled=...  32.1 us
    ppermute x1, waiting for transfers between devices, from_behind(): return lax.ppermute(block, axis, route)  23.7 us
    all_to_all x1, waiting for transfers between devices, body(): lax.all_to_all(pack(queries), 'dp', split_axis=0, concat_axis=0, tiled=True)  22.5 us
    all_to_all x1, starting transfers between devices, body(): lax.all_to_all(packed_grads.reshape(groups, per_peer, 3 * width), 'dp', s...  19.4 us
    all_to_all x1, starting transfers between devices, body(): lax.all_to_all(pack(grad_cells), 'dp', split_axis=0, concat_axis=0, tiled...  19.1 us
  transfers between devices with their start and end apart: 10, of which 7 were waited for; matrix products, arithmetic and copies ran while one was open for 6% of the time, Pallas kernels for 0%

commit v1 on v0

v1 whole, which is shorter than its diff:
```python
import jax
import jax.numpy as jnp
from jax import lax
from jax.sharding import PartitionSpec as P

HEADS = 20
HEAD_DIM = 128
CHUNKS = 1


def with_halo(value, axis, width):
    size, length = (lax.axis_size(axis), value.shape[0])
    up = [(i, (i + 1) % size) for i in range(size - 1)]
    down = [(j, i) for i, j in up]
    before = lax.ppermute(value[length - width :], axis, up)
    after = lax.ppermute(value[:width], axis, down)
    return jnp.concatenate([before, value, after], axis=0)


def passed_along(value, axis, steps):
    count = lax.axis_size(axis)
    initial, last = (max(0, -steps), min(count, count - steps))
    return lax.ppermute(value, axis, [(source, source + steps) for source in range(initial, last)])


def from_behind(block, axis, distance):
    devices = range(lax.axis_size(axis))
    route = [((i - distance) % len(devices), i) for i in devices]
    return lax.ppermute(block, axis, route)


def heads_of(matrix):
    return matrix.reshape(matrix.shape[0], -1, HEAD_DIM)


def chunk_grads(own_q, own_k, own_v, own_g, own_ids, window_ids, reach):
    cell_count, width = own_q.shape
    scale = HEAD_DIM ** (-0.5)
    key_value = jnp.concatenate([own_k, own_v], axis=1)
    key_value_window = with_halo(key_value, "dp", reach)
    key_window = key_value_window[:, :width]
    value_window = key_value_window[:, width:]
    scores = jnp.einsum(
        "ihd,jhd->hij", heads_of(own_q), heads_of(key_window), preferred_element_type=jnp.float32
    )
    scores = scores * scale
    allowed = (own_ids[:, None] == window_ids[None, :])[None]
    scores = jnp.where(allowed, scores, -jnp.inf)
    top = jnp.max(scores, axis=2)
    log_total = top + jnp.log(jnp.sum(jnp.exp(scores - top[:, :, None]), axis=2))
    probs = jnp.exp(scores - log_total[:, :, None])
    probs_low = probs.astype(jnp.bfloat16)
    grad_heads = heads_of(own_g)
    attended = jnp.einsum(
        "hij,jhd->ihd", probs_low, heads_of(value_window), preferred_element_type=jnp.float32
    )
    delta = jnp.sum(grad_heads.astype(jnp.float32) * attended, axis=2).T
    dprobs = jnp.einsum(
        "ihd,jhd->hij", grad_heads, heads_of(value_window), preferred_element_type=jnp.float32
    )
    dscores = (probs * (dprobs - delta[:, :, None]) * scale).astype(jnp.bfloat16)
    grad_query = jnp.einsum(
        "hij,jhd->ihd", dscores, heads_of(key_window), preferred_element_type=jnp.float32
    )
    grad_query = grad_query.reshape(cell_count, width).astype(jnp.bfloat16)
    window = cell_count + 2 * reach
    grad_key = jnp.einsum(
        "hij,ihd->jhd", dscores, heads_of(own_q), preferred_element_type=jnp.float32
    )
    grad_value = jnp.einsum(
        "hij,ihd->jhd", probs_low, grad_heads, preferred_element_type=jnp.float32
    )
    partial_value = jnp.concatenate(
        [grad_key.reshape(window, width), grad_value.reshape(window, width)], axis=1
    )
    from_after = passed_along(partial_value[:reach].astype(jnp.bfloat16), "dp", -1).astype(
        jnp.float32
    )
    from_before = passed_along(
        partial_value[reach + cell_count :].astype(jnp.bfloat16), "dp", 1
    ).astype(jnp.float32)
    summed = partial_value[reach : reach + cell_count]
    summed = summed.at[cell_count - reach :].add(from_after)
    summed = summed.at[:reach].add(from_before)
    return jnp.concatenate([grad_query, summed.astype(jnp.bfloat16)], axis=1)


def body(queries, key_cells, value_cells, grad_cells, packing, segment_ids):
    cell_count = queries.shape[1]
    width = queries.shape[2]
    groups = lax.axis_size("dp")
    per_peer = cell_count // groups
    reach = cell_count // 4
    place = lax.axis_index("dp")
    order = packing[0, 0]
    part = width // CHUNKS

    rim_ids = jnp.full((reach,), -1, jnp.int32)
    padded_ids = jnp.concatenate([rim_ids, segment_ids[0], rim_ids])
    window_ids = lax.dynamic_slice_in_dim(padded_ids, place * cell_count, cell_count + 2 * reach)
    own_ids = window_ids[reach : reach + cell_count]
    inverse = (
        jnp.zeros((cell_count,), jnp.int32).at[order].set(jnp.arange(cell_count, dtype=jnp.int32))
    )
    sources = (queries[0], key_cells[0], value_cells[0], grad_cells[0])
    pieces = []
    for c in range(CHUNKS):
        cols = slice(c * part, (c + 1) * part)
        stacked = jnp.concatenate([m[:, cols] for m in sources], axis=1)[order]
        arrived = lax.all_to_all(
            stacked.reshape(groups, per_peer, 4 * part), "dp", split_axis=0, concat_axis=0, tiled=True
        ).reshape(cell_count, 4 * part)
        own_q, own_k, own_v, own_g = [arrived[:, i * part : (i + 1) * part] for i in range(4)]
        packed_grads = chunk_grads(own_q, own_k, own_v, own_g, own_ids, window_ids, reach)
        returned = lax.all_to_all(
            packed_grads.reshape(groups, per_peer, 3 * part),
            "dp",
            split_axis=0,
            concat_axis=0,
            tiled=True,
        ).reshape(cell_count, 3 * part)
        pieces.append(from_behind(returned[inverse], "section", -1))
    ordered = [piece[:, i * part : (i + 1) * part] for i in range(3) for piece in pieces]
    return jnp.concatenate(ordered, axis=1)[None]


def solution(mesh):
    return jax.shard_map(
        body,
        mesh=mesh,
        in_specs=(
            P("section", "dp", None),
            P("section", "dp", None),
            P("section", "dp", None),
            P("section", "dp", None),
            P("section", "dp", None),
            P("section", None),
        ),
        out_specs=P("section", "dp", None),
        check_vma=False,
    )
```

time: 360 us -> 327 us (0.908)
  starting transfers between devices: 86.4 us -> 52.2 us
    all_to_all x5 -> x2, starting transfers between devices: 66.8 us -> 29.6 us  [the longest x1 19.5 us: body(): lax.all_to_all(stacked.reshape(groups, per_peer, 4 * part), 'dp', split_a...]
    ppermute x2, waiting for transfers between devices: 0.01 us -> 6.14 us  [the longest x1 4.54 us: with_halo(): after = lax.ppermute(value[:width], axis, down)]
    ppermute x2, starting transfers between devices: 5.02 us -> 9.43 us  [the longest x1 8.15 us: with_halo(): before = lax.ppermute(value[length - width:], axis, up)]
    all_to_all x5 -> x2, waiting for transfers between devices: 204 us -> 200 us  [the longest x1 116 us: body(): lax.all_to_all(stacked.reshape(groups, per_peer, 4 * part), 'dp', split_a...]
    reshape x8 -> x4, local copies, waits for them, and re-layouts: 13.3 us -> 13.7 us  [the longest x1 4.74 us: body(): stacked.reshape(groups, per_peer, 4 * part)]
  transfers between devices with their start and end apart: 10 -> 7, of which waited for: 7 -> 7; matrix products, arithmetic and copies ran while one was open for 6% -> 2% of each run, Pallas kernels for 0% -> 0%
where the time goes in v1:
time: 327 us; the launch traced here: 326 us
  waiting for transfers between devices  234 us (72%)
  starting transfers between devices  52.2 us (16%)
  local copies, waits for them, and re-layouts  30.6 us (9%)
  other arithmetic  5.92 us (2%)
  matrix products  3.48 us (1%)
    all_to_all x1, waiting for transfers between devices, body(): lax.all_to_all(stacked.reshape(groups, per_peer, 4 * part), 'dp', split_a...  116 us
    all_to_all x1, waiting for transfers between devices, body(): lax.all_to_all(packed_grads.reshape(groups, per_peer, 3 * part), 'dp', sp...  84.3 us
    ppermute x1, waiting for transfers between devices, from_behind(): return lax.ppermute(block, axis, route)  23.7 us
    all_to_all x1, starting transfers between devices, body(): lax.all_to_all(stacked.reshape(groups, per_peer, 4 * part), 'dp', split_a...  19.5 us
    all_to_all x1, starting transfers between devices, body(): lax.all_to_all(packed_grads.reshape(groups, per_peer, 3 * part), 'dp', sp...  10.2 us
    ppermute x1, starting transfers between devices, with_halo(): before = lax.ppermute(value[length - width:], axis, up)  8.15 us
    ppermute x1, starting transfers between devices, from_behind(): return lax.ppermute(block, axis, route)  7.88 us
  transfers between devices with their start and end apart: 7, of which 7 were waited for; matrix products, arithmetic and copies ran while one was open for 2% of the time, Pallas kernels for 0%

profile of v1, /device:TPU:1, one launch (start us, length us, event | category | flops | bytes accessed | tf_op | source)
XLA Modules:
  0.0 326.3 jit_solution(13086053720696081723)
XLA Ops:
  0.7 1.8 pad_maximum_fusion
  2.5 3.7 %gather_fusion = bf16[128,10240]{1,0:T(8,128)(2,1)} fusion(bf16[128,10240]{1,0:T(8,128)(2,1)S(1)} %pad_maximum_fusion, s32[1024]{0:T(1024)S(1)} %pad_clamp_fusion.1), kind=kCustom, calls=%fused_computation | custom fusion | bytes 5243392 | tf_op jit(solution)/shard_map/gather | solution.py:109
  6.2 4.7 %reshape.147 = bf16[64,2,10240]{2,1,0:T(2,128)(2,1)} reshape(bf16[128,10240]{1,0:T(8,128)(2,1)} %gather_fusion) | data formatting | bytes 5242880 | tf_op jit(solution)/shard_map/reshape | solution.py:111
  10.9 19.5 %all-to-all-start = ((bf16[64,2,10240]{2,1,0:T(2,128)(2,1)}), bf16[64,2,10240]{2,1,0:T(2,128)(2,1)}, u32[]{:S(2)}, u32[]{:S(2)}) async-start(bf16[64,2,10240]{2,1,0:T(2,128)(2,1)} %reshape.147), calls=%async_computation | async-start | bytes 5242880 | tf_op jit(solution)/shard_map/all_to_all | solution.py:110
  30.8 116.0 %all-to-all-done = bf16[64,2,10240]{2,1,0:T(2,128)(2,1)} async-done(((bf16[64,2,10240]{2,1,0:T(2,128)(2,1)}), bf16[64,2,10240]{2,1,0:T(2,128)(2,1)}, u32[]{:S(2)}, u32[]{:S(2)}) %all-to-all-start) | async-done | bytes 2621472 | tf_op jit(solution)/shard_map/all_to_all | solution.py:110
  146.8 3.0 reshape.148
  150.8 8.1 %collective-permute-start = (bf16[32,5120]{1,0:T(8,128)(2,1)}, bf16[32,5120]{1,0:T(8,128)(2,1)}, u32[]{:S(2)}, u32[]{:S(2)}) collective-permute-start(bf16[32,5120]{1,0:T(8,128)(2,1)} %get-tuple-element.31), channel_id=1, source_target_pairs={{0,1},{1,2},{2,3},{3,4},{4,5},{5,6},{6,7},{7,8},{8,9},{9,10},{10,1... | collective-permute-start | bytes 983048 | tf_op jit(solution)/shard_map/ppermute | solution.py:15
  158.9 1.3 collective-permute-start.1
  161.2 1.5 copy.26
  163.0 1.6 collective-permute-done
  164.6 4.5 %collective-permute-done.1 = bf16[32,5120]{1,0:T(8,128)(2,1)} collective-permute-done((bf16[32,5120]{1,0:T(8,128)(2,1)}, bf16[32,5120]{1,0:T(8,128)(2,1)}, u32[]{:S(2)}, u32[]{:S(2)}) %collective-permute-start.1) | collective-permute-done | bytes 327712 | tf_op jit(solution)/shard_map/ppermute | solution.py:16
  175.6 1.3 collective-permute-start.2
  178.8 4.0 %collective-permute-start.3 = (bf16[32,5120]{1,0:T(8,128)(2,1)}, bf16[32,5120]{1,0:T(8,128)(2,1)S(1)}, u32[]{:S(2)}, u32[]{:S(2)}) collective-permute-start(bf16[32,5120]{1,0:T(8,128)(2,1)} %get-tuple-element.33), channel_id=1, source_target_pairs={{0,1},{1,2},{2,3},{3,4},{4,5},{5,6},{6,7},{7,8},{8,9},{9,10},{10,1... | collective-permute-start | bytes 983048 | tf_op jit(solution)/shard_map/ppermute | solution.py:23
  182.8 2.2 collective-permute-done.2
  184.9 1.2 fusion.12
  186.1 1.5 collective-permute-done.3
  189.0 1.7 reshape.155
  190.7 10.2 %all-to-all-start.1 = ((bf16[64,2,7680]{2,1,0:T(2,128)(2,1)}), bf16[64,2,7680]{2,1,0:T(2,128)(2,1)}, u32[]{:S(2)}, u32[]{:S(2)}) async-start(bf16[64,2,7680]{2,1,0:T(2,128)(2,1)} %reshape.155), calls=%async_computation.1 | async-start | bytes 3932160 | tf_op jit(solution)/shard_map/all_to_all | solution.py:115
  201.9 84.3 %all-to-all-done.1 = bf16[64,2,7680]{2,1,0:T(2,128)(2,1)} async-done(((bf16[64,2,7680]{2,1,0:T(2,128)(2,1)}), bf16[64,2,7680]{2,1,0:T(2,128)(2,1)}, u32[]{:S(2)}, u32[]{:S(2)}) %all-to-all-start.1) | async-done | bytes 1966112 | tf_op jit(solution)/shard_map/all_to_all | solution.py:115
  286.2 4.2 %reshape.156 = bf16[128,7680]{1,0:T(8,128)(2,1)S(1)} reshape(bf16[64,2,7680]{2,1,0:T(2,128)(2,1)} %all-to-all-done.1) | data formatting | bytes 3932160 | tf_op jit(solution)/shard_map/reshape | solution.py:121
  290.4 3.1 gather_fusion.1
  293.5 7.9 %collective-permute-start.4 = (bf16[128,7680]{1,0:T(8,128)(2,1)}, bf16[128,7680]{1,0:T(8,128)(2,1)S(1)}, u32[]{:S(2)}, u32[]{:S(2)}) collective-permute-start(bf16[128,7680]{1,0:T(8,128)(2,1)} %gather_fusion.1), channel_id=1, source_target_pairs={{64,0},{128,64},{192,128},{256,192},{320,256},{384,320},{448,384},... | collective-permute-start | bytes 5898248 | tf_op jit(solution)/shard_map/ppermute | solution.py:29
  301.3 23.7 %collective-permute-done.4 = bf16[128,7680]{1,0:T(8,128)(2,1)S(1)} collective-permute-done((bf16[128,7680]{1,0:T(8,128)(2,1)}, bf16[128,7680]{1,0:T(8,128)(2,1)S(1)}, u32[]{:S(2)}, u32[]{:S(2)}) %collective-permute-start.4) | collective-permute-done | bytes 1966112 | tf_op jit(solution)/shard_map/ppermute | solution.py:29
  325.1 1.3 copy.68
  (43 shorter events, 13.8 us)
Async XLA Ops:
  10.9 19.5 %copy-start.3 = (s32[1,8192]{1,0:T(1,128)S(1)}, s32[1,8192]{1,0:T(1,128)}, u32[]{:S(2)}) copy-start(s32[1,8192]{1,0:T(1,128)} %param.15) | copy-start | bytes 98308
  10.9 135.9 %all-to-all-start = ((bf16[64,2,10240]{2,1,0:T(2,128)(2,1)}), bf16[64,2,10240]{2,1,0:T(2,128)(2,1)}, u32[]{:S(2)}, u32[]{:S(2)}) async-start(bf16[64,2,10240]{2,1,0:T(2,128)(2,1)} %reshape.147), calls=%async_computation | async-start | bytes 5242880 | tf_op jit(solution)/shard_map/all_to_all | solution.py:110
  149.8 11.4 %copy-start.1 = (bf16[128,10240]{1,0:T(8,128)(2,1)}, bf16[128,10240]{1,0:T(8,128)(2,1)S(1)}, u32[]{:S(2)}) copy-start(bf16[128,10240]{1,0:T(8,128)(2,1)S(1)} %reshape.148) | copy-start | bytes 7864324
  150.8 13.8 %collective-permute-start = (bf16[32,5120]{1,0:T(8,128)(2,1)}, bf16[32,5120]{1,0:T(8,128)(2,1)}, u32[]{:S(2)}, u32[]{:S(2)}) collective-permute-start(bf16[32,5120]{1,0:T(8,128)(2,1)} %get-tuple-element.31), channel_id=1, source_target_pairs={{0,1},{1,2},{2,3},{3,4},{4,5},{5,6},{6,7},{7,8},{8,9},{9,10},{10,1... | collective-permute-start | bytes 983048 | tf_op jit(solution)/shard_map/ppermute | solution.py:15
  158.9 10.2 %collective-permute-start.1 = (bf16[32,5120]{1,0:T(8,128)(2,1)}, bf16[32,5120]{1,0:T(8,128)(2,1)}, u32[]{:S(2)}, u32[]{:S(2)}) collective-permute-start(bf16[32,5120]{1,0:T(8,128)(2,1)} %get-tuple-element.32), channel_id=1, source_target_pairs={{1,0},{2,1},{3,2},{4,3},{5,4},{6,5},{7,6},{8,7},{9,8},{10,9},{11,1... | collective-permute-start | bytes 983048 | tf_op jit(solution)/shard_map/ppermute | solution.py:16
  161.2 8.0 %slice-start = ((bf16[128,10240]{1,0:T(8,128)(2,1)}), bf16[128,5120]{1,0:T(8,128)(2,1)S(1)}, s32[]{:S(2)}) async-start(bf16[128,10240]{1,0:T(8,128)(2,1)} %copy-done.1), calls=%async_computation.2 | async-start | bytes 2621440 | tf_op jit(solution)/shard_map/concatenate | solution.py:39
  174.2 2.7 copy-start
  175.6 9.3 %collective-permute-start.2 = (bf16[32,5120]{1,0:T(8,128)(2,1)}, bf16[32,5120]{1,0:T(8,128)(2,1)}, u32[]{:S(2)}, u32[]{:S(2)}) collective-permute-start(bf16[32,5120]{1,0:T(8,128)(2,1)} %get-tuple-element.34), channel_id=1, source_target_pairs={{1,0},{2,1},{3,2},{4,3},{5,4},{6,5},{7,6},{8,7},{9,8},{10,9},{11,1... | collective-permute-start | bytes 983048 | tf_op jit(solution)/shard_map/ppermute | solution.py:23
  178.8 8.9 %collective-permute-start.3 = (bf16[32,5120]{1,0:T(8,128)(2,1)}, bf16[32,5120]{1,0:T(8,128)(2,1)S(1)}, u32[]{:S(2)}, u32[]{:S(2)}) collective-permute-start(bf16[32,5120]{1,0:T(8,128)(2,1)} %get-tuple-element.33), channel_id=1, source_target_pairs={{0,1},{1,2},{2,3},{3,4},{4,5},{5,6},{6,7},{7,8},{8,9},{9,10},{10,1... | collective-permute-start | bytes 983048 | tf_op jit(solution)/shard_map/ppermute | solution.py:23
  187.8 1.1 copy-start.2
  190.7 95.4 %all-to-all-start.1 = ((bf16[64,2,7680]{2,1,0:T(2,128)(2,1)}), bf16[64,2,7680]{2,1,0:T(2,128)(2,1)}, u32[]{:S(2)}, u32[]{:S(2)}) async-start(bf16[64,2,7680]{2,1,0:T(2,128)(2,1)} %reshape.155), calls=%async_computation.1 | async-start | bytes 3932160 | tf_op jit(solution)/shard_map/all_to_all | solution.py:115
  293.5 31.6 %collective-permute-start.4 = (bf16[128,7680]{1,0:T(8,128)(2,1)}, bf16[128,7680]{1,0:T(8,128)(2,1)S(1)}, u32[]{:S(2)}, u32[]{:S(2)}) collective-permute-start(bf16[128,7680]{1,0:T(8,128)(2,1)} %gather_fusion.1), channel_id=1, source_target_pairs={{64,0},{128,64},{192,128},{256,192},{320,256},{384,320},{448,384},... | collective-permute-start | bytes 5898248 | tf_op jit(solution)/shard_map/ppermute | solution.py:29

commit v2 on v1

--- a/solution.py
+++ b/solution.py
@@ -5,7 +5,6 @@
 
 HEADS = 20
 HEAD_DIM = 128
-CHUNKS = 1
 
 
 def with_halo(value, axis, width):
@@ -82,7 +81,7 @@
     summed = partial_value[reach : reach + cell_count]
     summed = summed.at[cell_count - reach :].add(from_after)
     summed = summed.at[:reach].add(from_before)
-    return jnp.concatenate([grad_query, summed.astype(jnp.bfloat16)], axis=1)
+    return grad_query, summed.astype(jnp.bfloat16)
 
 
 def body(queries, key_cells, value_cells, grad_cells, packing, segment_ids):
@@ -93,35 +92,35 @@
     reach = cell_count // 4
     place = lax.axis_index("dp")
     order = packing[0, 0]
-    part = width // CHUNKS
 
     rim_ids = jnp.full((reach,), -1, jnp.int32)
     padded_ids = jnp.concatenate([rim_ids, segment_ids[0], rim_ids])
     window_ids = lax.dynamic_slice_in_dim(padded_ids, place * cell_count, cell_count + 2 * reach)
     own_ids = window_ids[reach : reach + cell_count]
-    inverse = (
-        jnp.zeros((cell_count,), jnp.int32).at[order].set(jnp.arange(cell_count, dtype=jnp.int32))
+    sources = (queries[0], key_cells[0], value_cells[0], grad_cells[0])
+    next_order = from_behind(order, "section", -1)
+    cells = jnp.arange(cell_count, dtype=jnp.int32)
+    picking = (order.reshape(groups, per_peer)[:, :, None] == cells).astype(jnp.bfloat16)
+    placing = (next_order.reshape(groups, per_peer)[None] == cells[:, None, None]).astype(jnp.bfloat16)
+    stacked = jnp.einsum(
+        "bgr,rf->bgf", picking, jnp.concatenate(sources, axis=1), preferred_element_type=jnp.float32
+    ).astype(jnp.bfloat16)
+    arrived = lax.all_to_all(stacked, "dp", split_axis=0, concat_axis=0, tiled=True)
+    arrived = arrived.reshape(cell_count, 4 * width)
+    own_q, own_k, own_v, own_g = [arrived[:, i * width : (i + 1) * width] for i in range(4)]
+    grad_query, summed = chunk_grads(own_q, own_k, own_v, own_g, own_ids, window_ids, reach)
+    next_query = from_behind(grad_query, "section", -1)
+    returned = lax.all_to_all(
+        jnp.concatenate([next_query, summed], axis=1).reshape(groups, per_peer, 3 * width),
+        "dp",
+        split_axis=0,
+        concat_axis=0,
+        tiled=True,
     )
-    sources = (queries[0], key_cells[0], value_cells[0], grad_cells[0])
-    pieces = []
-    for c in range(CHUNKS):
-        cols = slice(c * part, (c + 1) * part)
-        stacked = jnp.concatenate([m[:, cols] for m in sources], axis=1)[order]
-        arrived = lax.all_to_all(
-            stacked.reshape(groups, per_peer, 4 * part), "dp", split_axis=0, concat_axis=0, tiled=True
-        ).reshape(cell_count, 4 * part)
-        own_q, own_k, own_v, own_g = [arrived[:, i * part : (i + 1) * part] for i in range(4)]
-        packed_grads = chunk_grads(own_q, own_k, own_v, own_g, own_ids, window_ids, reach)
-        returned = lax.all_to_all(
-            packed_grads.reshape(groups, per_peer, 3 * part),
-            "dp",
-            split_axis=0,
-            concat_axis=0,
-            tiled=True,
-        ).reshape(cell_count, 3 * part)
-        pieces.append(from_behind(returned[inverse], "section", -1))
-    ordered = [piece[:, i * part : (i + 1) * part] for i in range(3) for piece in pieces]
-    return jnp.concatenate(ordered, axis=1)[None]
+    handed = from_behind(returned[:, :, width:], "section", -1)
+    arranged = jnp.concatenate([returned[:, :, :width], handed], axis=2)
+    loaded = jnp.einsum("kbg,bgf->kf", placing, arranged, preferred_element_type=jnp.float32)
+    return loaded.astype(jnp.bfloat16)[None]
 
 
 def solution(mesh):

time: 327 us -> 319 us (0.976)
  blocking collectives: 0 us -> 95.9 us
  waiting for transfers between devices: 234 us -> 144 us
  local copies, waits for them, and re-layouts: 30.6 us -> 18.5 us
  starting transfers between devices: 52.2 us -> 45.4 us
  matrix products: 3.48 us -> 9.44 us
    all_to_all x0 -> x1, blocking collectives: none -> 95.9 us  [body(): lax.all_to_all(jnp.concatenate([next_query, summed], axis=1).reshape(grou...]
    all_to_all x2 -> x1, waiting for transfers between devices: 200 us -> 116 us  [body(): lax.all_to_all(stacked, 'dp', split_axis=0, concat_axis=0, tiled=True)]
    all_to_all x2 -> x1, starting transfers between devices: 29.6 us -> 19.5 us  [body(): lax.all_to_all(stacked, 'dp', split_axis=0, concat_axis=0, tiled=True)]
    reshape x4 -> x2, local copies, waits for them, and re-layouts: 13.7 us -> 4.71 us  [the longest x1 2.99 us: body(): arrived = arrived.reshape(cell_count, 4 * width)]
    ppermute x1 -> x3, waiting for transfers between devices: 23.7 us -> 16.6 us  [from_behind(): return lax.ppermute(block, axis, route)]
    gather x2 -> x0, local copies, waits for them, and re-layouts: 6.81 us -> none  [the longest x1 3.73 us: body(): stacked = jnp.concatenate([m[:, cols] for m in sources], axis=1)[order]]
    dot_general x0 -> x2, matrix products: none -> 5.96 us  [the longest x1 3.38 us: body(): jnp.einsum('kbg,bgf->kf', placing, arranged, preferred_element_type=jnp.f...]
    convert_element_type x0 -> x1, local copies, waits for them, and re-layouts: none -> 4.2 us  [body(): stacked = jnp.einsum('bgr,rf->bgf', picking, jnp.concatenate(sources, axi...]
  transfers between devices with their start and end apart: 7 -> 8, of which waited for: 7 -> 5; matrix products, arithmetic and copies ran while one was open for 2% -> 2% of each run, Pallas kernels for 0% -> 0%
where the time goes in v2:
time: 319 us; the launch traced here: 318 us
  waiting for transfers between devices  144 us (45%)
  blocking collectives  95.9 us (30%)
  starting transfers between devices  45.4 us (14%)
  local copies, waits for them, and re-layouts  18.5 us (6%)
  matrix products  9.44 us (3%)
  other arithmetic  4.79 us (2%)
    all_to_all x1, waiting for transfers between devices, body(): lax.all_to_all(stacked, 'dp', split_axis=0, concat_axis=0, tiled=True)  116 us
    all_to_all x1, blocking collectives, body(): lax.all_to_all(jnp.concatenate([next_query, summed], axis=1).reshape(grou...  95.9 us
    all_to_all x1, starting transfers between devices, body(): lax.all_to_all(stacked, 'dp', split_axis=0, concat_axis=0, tiled=True)  19.5 us
    ppermute x3, waiting for transfers between devices, from_behind(): return lax.ppermute(block, axis, route)  16.6 us
    ppermute x3, starting transfers between devices, from_behind(): return lax.ppermute(block, axis, route)  10.9 us
    ppermute x1, starting transfers between devices, with_halo(): before = lax.ppermute(value[length - width:], axis, up)  8.18 us
  transfers between devices with their start and end apart: 8, of which 5 were waited for; matrix products, arithmetic and copies ran while one was open for 2% of the time, Pallas kernels for 0%

profile of v2, /device:TPU:1, one launch (start us, length us, event | category | flops | bytes accessed | tf_op | source)
XLA Modules:
  0.0 318.4 jit_solution(10722354677519191598)
XLA Ops:
  0.5 1.3 reduce.7
  2.0 2.6 convolution_convert_fusion
  4.6 4.2 %copy.30 = bf16[64,2,10240]{2,1,0:T(2,128)(2,1)} copy(bf16[64,2,10240]{2,0,1:T(8,128)(2,1)S(1)} %convolution_convert_fusion) | data formatting | bytes 5242880 | tf_op jit(solution)/shard_map/convert_element_type | solution.py:107
  8.8 19.5 %all-to-all-start = ((bf16[64,2,10240]{2,1,0:T(2,128)(2,1)}), bf16[64,2,10240]{2,1,0:T(2,128)(2,1)}, u32[]{:S(2)}, u32[]{:S(2)}) async-start(bf16[64,2,10240]{2,1,0:T(2,128)(2,1)} %copy.30), calls=%async_computation | async-start | bytes 5242880 | tf_op jit(solution)/shard_map/all_to_all | solution.py:108
  28.7 116.0 %all-to-all-done = bf16[64,2,10240]{2,1,0:T(2,128)(2,1)} async-done(((bf16[64,2,10240]{2,1,0:T(2,128)(2,1)}), bf16[64,2,10240]{2,1,0:T(2,128)(2,1)}, u32[]{:S(2)}, u32[]{:S(2)}) %all-to-all-start) | async-done | bytes 2621472 | tf_op jit(solution)/shard_map/all_to_all | solution.py:108
  144.7 3.0 reshape.115
  148.7 8.2 %collective-permute-start.1 = (bf16[32,5120]{1,0:T(8,128)(2,1)}, bf16[32,5120]{1,0:T(8,128)(2,1)}, u32[]{:S(2)}, u32[]{:S(2)}) collective-permute-start(bf16[32,5120]{1,0:T(8,128)(2,1)} %get-tuple-element.31), channel_id=1, source_target_pairs={{0,1},{1,2},{2,3},{3,4},{4,5},{5,6},{6,7},{7,8},{8,9},{9,10},{10,1... | collective-permute-start | bytes 983048 | tf_op jit(solution)/shard_map/ppermute | solution.py:14
  156.9 1.3 collective-permute-start.2
  159.1 1.5 copy.34
  160.9 1.6 collective-permute-done.1
  162.5 4.6 %collective-permute-done.2 = bf16[32,5120]{1,0:T(8,128)(2,1)} collective-permute-done((bf16[32,5120]{1,0:T(8,128)(2,1)}, bf16[32,5120]{1,0:T(8,128)(2,1)}, u32[]{:S(2)}, u32[]{:S(2)}) %collective-permute-start.2) | collective-permute-done | bytes 327712 | tf_op jit(solution)/shard_map/ppermute | solution.py:15
  167.1 1.2 pad_maximum_fusion
  172.4 1.1 fusion.32
  173.6 1.3 collective-permute-start.4
  175.6 1.1 copy.39
  176.7 2.1 collective-permute-start.3
  178.8 4.3 %collective-permute-start.5 = (bf16[32,5120]{1,0:T(8,128)(2,1)}, bf16[32,5120]{1,0:T(8,128)(2,1)S(1)}, u32[]{:S(2)}, u32[]{:S(2)}) collective-permute-start(bf16[32,5120]{1,0:T(8,128)(2,1)} %get-tuple-element.33), channel_id=1, source_target_pairs={{0,1},{1,2},{2,3},{3,4},{4,5},{5,6},{6,7},{7,8},{8,9},{9,10},{10,1... | collective-permute-start | bytes 983048 | tf_op jit(solution)/shard_map/ppermute | solution.py:22
  183.1 1.2 fusion.23
  184.3 5.3 %collective-permute-done.5 = bf16[32,5120]{1,0:T(8,128)(2,1)S(1)} collective-permute-done((bf16[32,5120]{1,0:T(8,128)(2,1)}, bf16[32,5120]{1,0:T(8,128)(2,1)S(1)}, u32[]{:S(2)}, u32[]{:S(2)}) %collective-permute-start.5) | collective-permute-done | bytes 327712 | tf_op jit(solution)/shard_map/ppermute | solution.py:22
  190.1 1.7 reshape.122
  191.8 95.9 %all_to_all.10 = bf16[64,2,7680]{2,1,0:T(2,128)(2,1)S(1)} all-to-all(bf16[64,2,7680]{2,1,0:T(2,128)(2,1)} %reshape.122), channel_id=1, replica_groups=mesh['section'=8,'dp'=64] {'dp'}, dimensions={0} | all-to-all | bytes 3932160 | tf_op jit(solution)/shard_map/all_to_all | solution.py:113
  288.9 8.4 %collective-permute-start.6 = (bf16[64,2,5120]{2,0,1:T(8,128)(2,1)S(1)}, bf16[64,2,5120]{2,0,1:T(8,128)(2,1)}, u32[]{:S(2)}, u32[]{:S(2)}) collective-permute-start(bf16[64,2,5120]{2,0,1:T(8,128)(2,1)S(1)} %copy.51), channel_id=1, source_target_pairs={{64,0},{128,64},{192,128},{256,192},{320,256},{384,320},{448,384},... | collective-permute-start | bytes 3932168 | tf_op jit(solution)/shard_map/ppermute | solution.py:28
  297.7 16.6 %collective-permute-done = s32[128]{0:T(128)S(1)} collective-permute-done((s32[128]{0:T(128)S(1)}, s32[128]{0:T(128)S(1)}, u32[]{:S(2)}, u32[]{:S(2)}) %collective-permute-start) | collective-permute-done | bytes 544 | tf_op jit(solution)/shard_map/ppermute | solution.py:28
  315.0 3.4 %fusion.1 = bf16[1,128,7680]{2,1,0:T(8,128)(2,1)} fusion(bf16[64,2,5120]{2,0,1:T(8,128)(2,1)} %collective-permute-done.6, bf16[64,2,2560]{2,0,1:T(8,128)(2,1)S(1)} %copy.50, s32[64,2]{0,1:T(2,128)S(1)} %copy.28), kind=kOutput, calls=%fused_computation.3 | convolution fusion | flops 256589824 | bytes 3932672 | tf_op jit(solution)/shard_map/kbg,bgf->kf/dot_general | solution.py:122
  (47 shorter events, 10.8 us)
Async XLA Ops:
  8.8 19.5 %copy-start.2 = (s32[1,8192]{1,0:T(1,128)S(1)}, s32[1,8192]{1,0:T(1,128)}, u32[]{:S(2)}) copy-start(s32[1,8192]{1,0:T(1,128)} %param.15) | copy-start | bytes 98308
  8.8 135.9 %all-to-all-start = ((bf16[64,2,10240]{2,1,0:T(2,128)(2,1)}), bf16[64,2,10240]{2,1,0:T(2,128)(2,1)}, u32[]{:S(2)}, u32[]{:S(2)}) async-start(bf16[64,2,10240]{2,1,0:T(2,128)(2,1)} %copy.30), calls=%async_computation | async-start | bytes 5242880 | tf_op jit(solution)/shard_map/all_to_all | solution.py:108
  147.7 11.4 %copy-start.1 = (bf16[128,10240]{1,0:T(8,128)(2,1)}, bf16[128,10240]{1,0:T(8,128)(2,1)S(1)}, u32[]{:S(2)}) copy-start(bf16[128,10240]{1,0:T(8,128)(2,1)S(1)} %reshape.115) | copy-start | bytes 7864324
  148.7 13.8 %collective-permute-start.1 = (bf16[32,5120]{1,0:T(8,128)(2,1)}, bf16[32,5120]{1,0:T(8,128)(2,1)}, u32[]{:S(2)}, u32[]{:S(2)}) collective-permute-start(bf16[32,5120]{1,0:T(8,128)(2,1)} %get-tuple-element.31), channel_id=1, source_target_pairs={{0,1},{1,2},{2,3},{3,4},{4,5},{5,6},{6,7},{7,8},{8,9},{9,10},{10,1... | collective-permute-start | bytes 983048 | tf_op jit(solution)/shard_map/ppermute | solution.py:14
  156.9 10.2 %collective-permute-start.2 = (bf16[32,5120]{1,0:T(8,128)(2,1)}, bf16[32,5120]{1,0:T(8,128)(2,1)}, u32[]{:S(2)}, u32[]{:S(2)}) collective-permute-start(bf16[32,5120]{1,0:T(8,128)(2,1)} %get-tuple-element.32), channel_id=1, source_target_pairs={{1,0},{2,1},{3,2},{4,3},{5,4},{6,5},{7,6},{8,7},{9,8},{10,9},{11,1... | collective-permute-start | bytes 983048 | tf_op jit(solution)/shard_map/ppermute | solution.py:15
  159.1 8.0 %slice-start = ((bf16[128,10240]{1,0:T(8,128)(2,1)}), bf16[128,5120]{1,0:T(8,128)(2,1)S(1)}, s32[]{:S(2)}) async-start(bf16[128,10240]{1,0:T(8,128)(2,1)} %copy-done.1), calls=%async_computation.2 | async-start | bytes 2621440 | tf_op jit(solution)/shard_map/concatenate | solution.py:38
  172.1 2.7 copy-start
  173.6 9.5 %collective-permute-start.4 = (bf16[32,5120]{1,0:T(8,128)(2,1)}, bf16[32,5120]{1,0:T(8,128)(2,1)}, u32[]{:S(2)}, u32[]{:S(2)}) collective-permute-start(bf16[32,5120]{1,0:T(8,128)(2,1)} %get-tuple-element.34), channel_id=1, source_target_pairs={{1,0},{2,1},{3,2},{4,3},{5,4},{6,5},{7,6},{8,7},{9,8},{10,9},{11,1... | collective-permute-start | bytes 983048 | tf_op jit(solution)/shard_map/ppermute | solution.py:22
  176.7 13.2 %collective-permute-start.3 = (bf16[128,2560]{1,0:T(8,128)(2,1)}, bf16[128,2560]{1,0:T(8,128)(2,1)S(1)}, u32[]{:S(2)}, u32[]{:S(2)}) collective-permute-start(bf16[128,2560]{1,0:T(8,128)(2,1)} %copy.39), channel_id=1, source_target_pairs={{64,0},{128,64},{192,128},{256,192},{320,256},{384,320},{448,384},... | collective-permute-start | bytes 1966088 | tf_op jit(solution)/shard_map/ppermute | solution.py:28
  178.8 10.9 %collective-permute-start.5 = (bf16[32,5120]{1,0:T(8,128)(2,1)}, bf16[32,5120]{1,0:T(8,128)(2,1)S(1)}, u32[]{:S(2)}, u32[]{:S(2)}) collective-permute-start(bf16[32,5120]{1,0:T(8,128)(2,1)} %get-tuple-element.33), channel_id=1, source_target_pairs={{0,1},{1,2},{2,3},{3,4},{4,5},{5,6},{6,7},{7,8},{8,9},{9,10},{10,1... | collective-permute-start | bytes 983048 | tf_op jit(solution)/shard_map/ppermute | solution.py:22
  288.7 8.7 %copy-start.3 = (s32[1,1,128]{2,1,0:T(1,128)S(1)}, s32[1,1,128]{2,1,0:T(1,128)}, u32[]{:S(2)}) copy-start(s32[1,1,128]{2,1,0:T(1,128)} %param.14) | copy-start | bytes 1540
  288.9 26.1 %collective-permute-start.6 = (bf16[64,2,5120]{2,0,1:T(8,128)(2,1)S(1)}, bf16[64,2,5120]{2,0,1:T(8,128)(2,1)}, u32[]{:S(2)}, u32[]{:S(2)}) collective-permute-start(bf16[64,2,5120]{2,0,1:T(8,128)(2,1)S(1)} %copy.51), channel_id=1, source_target_pairs={{64,0},{128,64},{192,128},{256,192},{320,256},{384,320},{448,384},... | collective-permute-start | bytes 3932168 | tf_op jit(solution)/shard_map/ppermute | solution.py:28
  297.3 16.9 %collective-permute-start = (s32[128]{0:T(128)S(1)}, s32[128]{0:T(128)S(1)}, u32[]{:S(2)}, u32[]{:S(2)}) collective-permute-start(s32[128]{0:T(128)S(1)} %bitcast.73), channel_id=1, source_target_pairs={{64,0},{128,64},{192,128},{256,192},{320,256},{384,320},{448,384},... | collective-permute-start | bytes 1544 | tf_op jit(solution)/shard_map/ppermute | solution.py:28

commit v3 on v2

--- a/solution.py
+++ b/solution.py
@@ -7,12 +7,13 @@
 HEAD_DIM = 128
 
 
-def with_halo(value, axis, width):
-    size, length = (lax.axis_size(axis), value.shape[0])
-    up = [(i, (i + 1) % size) for i in range(size - 1)]
+def with_halo(value, edges, axis):
+    size = lax.axis_size(axis)
+    up = [(i, i + 1) for i in range(size - 1)]
     down = [(j, i) for i, j in up]
-    before = lax.ppermute(value[length - width :], axis, up)
-    after = lax.ppermute(value[:width], axis, down)
+    head, tail = edges
+    before = lax.ppermute(tail, axis, up)
+    after = lax.ppermute(head, axis, down)
     return jnp.concatenate([before, value, after], axis=0)
 
 
@@ -32,11 +33,11 @@
     return matrix.reshape(matrix.shape[0], -1, HEAD_DIM)
 
 
-def chunk_grads(own_q, own_k, own_v, own_g, own_ids, window_ids, reach):
+def chunk_grads(own_q, own_k, own_v, own_g, edges, own_ids, window_ids, reach):
     cell_count, width = own_q.shape
     scale = HEAD_DIM ** (-0.5)
     key_value = jnp.concatenate([own_k, own_v], axis=1)
-    key_value_window = with_halo(key_value, "dp", reach)
+    key_value_window = with_halo(key_value, edges, "dp")
     key_window = key_value_window[:, :width]
     value_window = key_value_window[:, width:]
     scores = jnp.einsum(
@@ -106,9 +107,16 @@
         "bgr,rf->bgf", picking, jnp.concatenate(sources, axis=1), preferred_element_type=jnp.float32
     ).astype(jnp.bfloat16)
     arrived = lax.all_to_all(stacked, "dp", split_axis=0, concat_axis=0, tiled=True)
+    edge_blocks = reach // per_peer
+    edges = (
+        arrived[:edge_blocks, :, width : 3 * width].reshape(reach, 2 * width),
+        arrived[groups - edge_blocks :, :, width : 3 * width].reshape(reach, 2 * width),
+    )
     arrived = arrived.reshape(cell_count, 4 * width)
     own_q, own_k, own_v, own_g = [arrived[:, i * width : (i + 1) * width] for i in range(4)]
-    grad_query, summed = chunk_grads(own_q, own_k, own_v, own_g, own_ids, window_ids, reach)
+    grad_query, summed = chunk_grads(
+        own_q, own_k, own_v, own_g, edges, own_ids, window_ids, reach
+    )
     next_query = from_behind(grad_query, "section", -1)
     returned = lax.all_to_all(
         jnp.concatenate([next_query, summed], axis=1).reshape(groups, per_peer, 3 * width),

time: 319 us -> 316 us (level)
  waiting for transfers between devices: 144 us -> 138 us
    ppermute x2, waiting for transfers between devices: 6.15 us -> 0.41 us  [the longest x1 0.41 us: with_halo(): before = lax.ppermute(tail, axis, up)]
  transfers between devices with their start and end apart: 8 -> 8, of which waited for: 5 -> 4; matrix products, arithmetic and copies ran while one was open for 2% -> 3% of each run, Pallas kernels for 0% -> 0%
where the time goes in v3:
time: 316 us
  waiting for transfers between devices  138 us (44%)
  blocking collectives  97.6 us (31%)
  starting transfers between devices  46.6 us (15%)
  local copies, waits for them, and re-layouts  18.6 us (6%)
  matrix products  9.44 us (3%)
  other arithmetic  4.79 us (2%)
    all_to_all x1, waiting for transfers between devices, body(): lax.all_to_all(stacked, 'dp', split_axis=0, concat_axis=0, tiled=True)  116 us
    all_to_all x1, blocking collectives, body(): lax.all_to_all(jnp.concatenate([next_query, summed], axis=1).reshape(grou...  97.6 us
    all_to_all x1, starting transfers between devices, body(): lax.all_to_all(stacked, 'dp', split_axis=0, concat_axis=0, tiled=True)  19.2 us
    ppermute x3, waiting for transfers between devices, from_behind(): return lax.ppermute(block, axis, route)  16.4 us
    ppermute x3, starting transfers between devices, from_behind(): return lax.ppermute(block, axis, route)  11 us
    ppermute x1, starting transfers between devices, with_halo(): before = lax.ppermute(tail, axis, up)  8.82 us
  transfers between devices with their start and end apart: 8, of which 4 were waited for; matrix products, arithmetic and copies ran while one was open for 3% of the time, Pallas kernels for 0%

profile of v3, /device:TPU:1, one launch (start us, length us, event | category | flops | bytes accessed | tf_op | source)
XLA Modules:
  0.0 315.7 jit_solution(1264817849591503498)
XLA Ops:
  0.5 1.3 reduce.7
  2.0 2.6 convolution_convert_fusion
  4.6 4.2 %copy.32 = bf16[64,2,10240]{2,1,0:T(2,128)(2,1)} copy(bf16[64,2,10240]{2,0,1:T(8,128)(2,1)S(1)} %convolution_convert_fusion) | data formatting | bytes 5242880 | tf_op jit(solution)/shard_map/convert_element_type | solution.py:108
  8.8 19.2 %all-to-all-start = ((bf16[64,2,10240]{2,1,0:T(2,128)(2,1)}), bf16[64,2,10240]{2,1,0:T(2,128)(2,1)S(1)}, u32[]{:S(2)}, u32[]{:S(2)}) async-start(bf16[64,2,10240]{2,1,0:T(2,128)(2,1)} %copy.32), calls=%async_computation | async-start | bytes 5242880 | tf_op jit(solution)/shard_map/all_to_all | solution.py:109
  28.5 116.1 %all-to-all-done = bf16[64,2,10240]{2,1,0:T(2,128)(2,1)S(1)} async-done(((bf16[64,2,10240]{2,1,0:T(2,128)(2,1)}), bf16[64,2,10240]{2,1,0:T(2,128)(2,1)S(1)}, u32[]{:S(2)}, u32[]{:S(2)}) %all-to-all-start) | async-done | bytes 2621472 | tf_op jit(solution)/shard_map/all_to_all | solution.py:109
  145.1 0.9 reshape.121
  146.8 1.3 collective-permute-start.2
  148.0 8.8 %collective-permute-start.1 = (bf16[32,5120]{1,0:T(8,128)(2,1)}, bf16[32,5120]{1,0:T(8,128)(2,1)}, u32[]{:S(2)}, u32[]{:S(2)}) collective-permute-start(bf16[32,5120]{1,0:T(8,128)(2,1)} %reshape.121), channel_id=1, source_target_pairs={{0,1},{1,2},{2,3},{3,4},{4,5},{5,6},{6,7},{7,8},{8,9},{9,10},{10,1... | collective-permute-start | bytes 983048 | tf_op jit(solution)/shard_map/ppermute | solution.py:15
  156.9 2.4 reshape.122
  159.3 1.4 fusion.30
  162.0 1.2 pad_maximum_fusion
  167.3 1.1 fusion.32
  168.4 1.3 collective-permute-start.4
  170.5 1.1 copy.41
  171.6 2.4 collective-permute-start.3
  173.9 4.9 %collective-permute-start.5 = (bf16[32,5120]{1,0:T(8,128)(2,1)}, bf16[32,5120]{1,0:T(8,128)(2,1)S(1)}, u32[]{:S(2)}, u32[]{:S(2)}) collective-permute-start(bf16[32,5120]{1,0:T(8,128)(2,1)} %get-tuple-element.33), channel_id=1, source_target_pairs={{0,1},{1,2},{2,3},{3,4},{4,5},{5,6},{6,7},{7,8},{8,9},{9,10},{10,1... | collective-permute-start | bytes 983048 | tf_op jit(solution)/shard_map/ppermute | solution.py:23
  178.9 1.2 fusion.23
  180.1 5.4 %collective-permute-done.5 = bf16[32,5120]{1,0:T(8,128)(2,1)S(1)} collective-permute-done((bf16[32,5120]{1,0:T(8,128)(2,1)}, bf16[32,5120]{1,0:T(8,128)(2,1)S(1)}, u32[]{:S(2)}, u32[]{:S(2)}) %collective-permute-start.5) | collective-permute-done | bytes 327712 | tf_op jit(solution)/shard_map/ppermute | solution.py:23
  185.9 1.7 reshape.130
  187.6 97.6 %all_to_all.10 = bf16[64,2,7680]{2,1,0:T(2,128)(2,1)S(1)} all-to-all(bf16[64,2,7680]{2,1,0:T(2,128)(2,1)} %reshape.130), channel_id=1, replica_groups=mesh['section'=8,'dp'=64] {'dp'}, dimensions={0} | all-to-all | bytes 3932160 | tf_op jit(solution)/shard_map/all_to_all | solution.py:121
  285.2 0.9 slice.106
  286.4 8.3 %collective-permute-start.6 = (bf16[64,2,5120]{2,0,1:T(8,128)(2,1)S(1)}, bf16[64,2,5120]{2,0,1:T(8,128)(2,1)}, u32[]{:S(2)}, u32[]{:S(2)}) collective-permute-start(bf16[64,2,5120]{2,0,1:T(8,128)(2,1)S(1)} %copy.53), channel_id=1, source_target_pairs={{64,0},{128,64},{192,128},{256,192},{320,256},{384,320},{448,384},... | collective-permute-start | bytes 3932168 | tf_op jit(solution)/shard_map/ppermute | solution.py:29
  295.1 16.4 %collective-permute-done = s32[128]{0:T(128)S(1)} collective-permute-done((s32[128]{0:T(128)S(1)}, s32[128]{0:T(128)S(1)}, u32[]{:S(2)}, u32[]{:S(2)}) %collective-permute-start) | collective-permute-done | bytes 544 | tf_op jit(solution)/shard_map/ppermute | solution.py:29
  312.3 3.4 %fusion.1 = bf16[1,128,7680]{2,1,0:T(8,128)(2,1)} fusion(bf16[64,2,5120]{2,0,1:T(8,128)(2,1)} %collective-permute-done.6, bf16[64,2,2560]{2,0,1:T(8,128)(2,1)S(1)} %copy.52, s32[64,2]{0,1:T(2,128)S(1)} %copy.30), kind=kOutput, calls=%fused_computation.3 | convolution fusion | flops 256589824 | bytes 3932672 | tf_op jit(solution)/shard_map/kbg,bgf->kf/dot_general | solution.py:130
  (47 shorter events, 10.2 us)
Async XLA Ops:
  8.8 19.3 %copy-start.1 = (s32[1,8192]{1,0:T(1,128)S(1)}, s32[1,8192]{1,0:T(1,128)}, u32[]{:S(2)}) copy-start(s32[1,8192]{1,0:T(1,128)} %param.15) | copy-start | bytes 98308
  8.8 135.8 %all-to-all-start = ((bf16[64,2,10240]{2,1,0:T(2,128)(2,1)}), bf16[64,2,10240]{2,1,0:T(2,128)(2,1)S(1)}, u32[]{:S(2)}, u32[]{:S(2)}) async-start(bf16[64,2,10240]{2,1,0:T(2,128)(2,1)} %copy.32), calls=%async_computation | async-start | bytes 5242880 | tf_op jit(solution)/shard_map/all_to_all | solution.py:109
  146.8 14.6 %collective-permute-start.2 = (bf16[32,5120]{1,0:T(8,128)(2,1)}, bf16[32,5120]{1,0:T(8,128)(2,1)}, u32[]{:S(2)}, u32[]{:S(2)}) collective-permute-start(bf16[32,5120]{1,0:T(8,128)(2,1)} %reshape.123), channel_id=1, source_target_pairs={{1,0},{2,1},{3,2},{4,3},{5,4},{6,5},{7,6},{8,7},{9,8},{10,9},{11,1... | collective-permute-start | bytes 983048 | tf_op jit(solution)/shard_map/ppermute | solution.py:16
  148.0 13.7 %collective-permute-start.1 = (bf16[32,5120]{1,0:T(8,128)(2,1)}, bf16[32,5120]{1,0:T(8,128)(2,1)}, u32[]{:S(2)}, u32[]{:S(2)}) collective-permute-start(bf16[32,5120]{1,0:T(8,128)(2,1)} %reshape.121), channel_id=1, source_target_pairs={{0,1},{1,2},{2,3},{3,4},{4,5},{5,6},{6,7},{7,8},{8,9},{9,10},{10,1... | collective-permute-start | bytes 983048 | tf_op jit(solution)/shard_map/ppermute | solution.py:15
  160.7 1.3 slice-start
  167.0 2.7 copy-start
  168.4 10.4 %collective-permute-start.4 = (bf16[32,5120]{1,0:T(8,128)(2,1)}, bf16[32,5120]{1,0:T(8,128)(2,1)}, u32[]{:S(2)}, u32[]{:S(2)}) collective-permute-start(bf16[32,5120]{1,0:T(8,128)(2,1)} %get-tuple-element.34), channel_id=1, source_target_pairs={{1,0},{2,1},{3,2},{4,3},{5,4},{6,5},{7,6},{8,7},{9,8},{10,9},{11,1... | collective-permute-start | bytes 983048 | tf_op jit(solution)/shard_map/ppermute | solution.py:23
  171.6 14.2 %collective-permute-start.3 = (bf16[128,2560]{1,0:T(8,128)(2,1)}, bf16[128,2560]{1,0:T(8,128)(2,1)S(1)}, u32[]{:S(2)}, u32[]{:S(2)}) collective-permute-start(bf16[128,2560]{1,0:T(8,128)(2,1)} %copy.41), channel_id=1, source_target_pairs={{64,0},{128,64},{192,128},{256,192},{320,256},{384,320},{448,384},... | collective-permute-start | bytes 1966088 | tf_op jit(solution)/shard_map/ppermute | solution.py:29
  173.9 11.5 %collective-permute-start.5 = (bf16[32,5120]{1,0:T(8,128)(2,1)}, bf16[32,5120]{1,0:T(8,128)(2,1)S(1)}, u32[]{:S(2)}, u32[]{:S(2)}) collective-permute-start(bf16[32,5120]{1,0:T(8,128)(2,1)} %get-tuple-element.33), channel_id=1, source_target_pairs={{0,1},{1,2},{2,3},{3,4},{4,5},{5,6},{6,7},{7,8},{8,9},{9,10},{10,1... | collective-permute-start | bytes 983048 | tf_op jit(solution)/shard_map/ppermute | solution.py:23
  286.1 8.6 %copy-start.2 = (s32[1,1,128]{2,1,0:T(1,128)S(1)}, s32[1,1,128]{2,1,0:T(1,128)}, u32[]{:S(2)}) copy-start(s32[1,1,128]{2,1,0:T(1,128)} %param.14) | copy-start | bytes 1540
  286.4 25.9 %collective-permute-start.6 = (bf16[64,2,5120]{2,0,1:T(8,128)(2,1)S(1)}, bf16[64,2,5120]{2,0,1:T(8,128)(2,1)}, u32[]{:S(2)}, u32[]{:S(2)}) collective-permute-start(bf16[64,2,5120]{2,0,1:T(8,128)(2,1)S(1)} %copy.53), channel_id=1, source_target_pairs={{64,0},{128,64},{192,128},{256,192},{320,256},{384,320},{448,384},... | collective-permute-start | bytes 3932168 | tf_op jit(solution)/shard_map/ppermute | solution.py:29
  294.7 16.8 %collective-permute-start = (s32[128]{0:T(128)S(1)}, s32[128]{0:T(128)S(1)}, u32[]{:S(2)}, u32[]{:S(2)}) collective-permute-start(s32[128]{0:T(128)S(1)} %bitcast.73), channel_id=1, source_target_pairs={{64,0},{128,64},{192,128},{256,192},{320,256},{384,320},{448,384},... | collective-permute-start | bytes 1544 | tf_op jit(solution)/shard_map/ppermute | solution.py:29

commit v4 on v3

--- a/solution.py
+++ b/solution.py
@@ -12,8 +12,8 @@
     up = [(i, i + 1) for i in range(size - 1)]
     down = [(j, i) for i, j in up]
     head, tail = edges
-    before = lax.ppermute(tail, axis, up)
-    after = lax.ppermute(head, axis, down)
+    before = lax.ppermute(tail, axis, up).reshape(-1, value.shape[1])
+    after = lax.ppermute(head, axis, down).reshape(-1, value.shape[1])
     return jnp.concatenate([before, value, after], axis=0)
 
 
@@ -109,8 +109,8 @@
     arrived = lax.all_to_all(stacked, "dp", split_axis=0, concat_axis=0, tiled=True)
     edge_blocks = reach // per_peer
     edges = (
-        arrived[:edge_blocks, :, width : 3 * width].reshape(reach, 2 * width),
-        arrived[groups - edge_blocks :, :, width : 3 * width].reshape(reach, 2 * width),
+        arrived[:edge_blocks, :, width : 3 * width],
+        arrived[groups - edge_blocks :, :, width : 3 * width],
     )
     arrived = arrived.reshape(cell_count, 4 * width)
     own_q, own_k, own_v, own_g = [arrived[:, i * width : (i + 1) * width] for i in range(4)]

time: 316 us -> 316 us (level)
  no operation moved by 1% of the time
where the time goes in v4:
time: 316 us; the launch traced here: 315 us
  waiting for transfers between devices  141 us (45%)
  blocking collectives  95.8 us (30%)
  starting transfers between devices  45.3 us (14%)
  local copies, waits for them, and re-layouts  19.7 us (6%)
  matrix products  9.44 us (3%)
  other arithmetic  3.72 us (1%)
    all_to_all x1, waiting for transfers between devices, body(): lax.all_to_all(stacked, 'dp', split_axis=0, concat_axis=0, tiled=True)  116 us
    all_to_all x1, blocking collectives, body(): lax.all_to_all(jnp.concatenate([next_query, summed], axis=1).reshape(grou...  95.8 us
    all_to_all x1, starting transfers between devices, body(): lax.all_to_all(stacked, 'dp', split_axis=0, concat_axis=0, tiled=True)  19.2 us
    ppermute x3, waiting for transfers between devices, from_behind(): return lax.ppermute(block, axis, route)  16.6 us
    ppermute x3, starting transfers between devices, from_behind(): return lax.ppermute(block, axis, route)  10.9 us
    ppermute x1, starting transfers between devices, with_halo(): before = lax.ppermute(tail, axis, up).reshape(-1, value.shape[1])  8.15 us
  transfers between devices with their start and end apart: 8, of which 4 were waited for; matrix products, arithmetic and copies ran while one was open for 3% of the time, Pallas kernels for 0%

profile of v4, /device:TPU:1, one launch (start us, length us, event | category | flops | bytes accessed | tf_op | source)
XLA Modules:
  0.0 315.5 jit_solution(1191878463310322739)
XLA Ops:
  0.5 1.3 reduce.7
  2.0 2.6 convolution_convert_fusion
  4.6 4.2 %copy.32 = bf16[64,2,10240]{2,1,0:T(2,128)(2,1)} copy(bf16[64,2,10240]{2,0,1:T(8,128)(2,1)S(1)} %convolution_convert_fusion) | data formatting | bytes 5242880 | tf_op jit(solution)/shard_map/convert_element_type | solution.py:108
  8.8 19.2 %all-to-all-start = ((bf16[64,2,10240]{2,1,0:T(2,128)(2,1)}), bf16[64,2,10240]{2,1,0:T(2,128)(2,1)S(1)}, u32[]{:S(2)}, u32[]{:S(2)}) async-start(bf16[64,2,10240]{2,1,0:T(2,128)(2,1)} %copy.32), calls=%async_computation | async-start | bytes 5242880 | tf_op jit(solution)/shard_map/all_to_all | solution.py:109
  28.5 116.1 %all-to-all-done = bf16[64,2,10240]{2,1,0:T(2,128)(2,1)S(1)} async-done(((bf16[64,2,10240]{2,1,0:T(2,128)(2,1)}), bf16[64,2,10240]{2,1,0:T(2,128)(2,1)S(1)}, u32[]{:S(2)}, u32[]{:S(2)}) %all-to-all-start) | async-done | bytes 2621472 | tf_op jit(solution)/shard_map/all_to_all | solution.py:109
  144.6 1.3 fusion.31
  145.9 8.1 %collective-permute-start.1 = (bf16[16,2,5120]{2,1,0:T(2,128)(2,1)}, bf16[16,2,5120]{2,1,0:T(2,128)(2,1)}, u32[]{:S(2)}, u32[]{:S(2)}) collective-permute-start(bf16[16,2,5120]{2,1,0:T(2,128)(2,1)} %get-tuple-element.31), channel_id=1, source_target_pairs={{0,1},{1,2},{2,3},{3,4},{4,5},{5,6},{6,7},{7,8},{8,9},{9,10},{10,1... | collective-permute-start | bytes 983048 | tf_op jit(solution)/shard_map/ppermute | solution.py:15
  154.1 1.3 collective-permute-start.2
  155.3 2.4 reshape.122
  157.8 1.4 fusion.30
  159.8 1.1 reshape.121
  160.9 3.3 %collective-permute-done.2 = bf16[16,2,5120]{2,1,0:T(2,128)(2,1)} collective-permute-done((bf16[16,2,5120]{2,1,0:T(2,128)(2,1)}, bf16[16,2,5120]{2,1,0:T(2,128)(2,1)}, u32[]{:S(2)}, u32[]{:S(2)}) %collective-permute-start.2) | collective-permute-done | bytes 327712 | tf_op jit(solution)/shard_map/ppermute | solution.py:16
  164.3 1.1 reshape.123
  169.6 1.1 fusion.32
  170.8 1.3 collective-permute-start.4
  173.9 2.1 collective-permute-start.3
  176.0 4.5 %collective-permute-start.5 = (bf16[32,5120]{1,0:T(8,128)(2,1)}, bf16[32,5120]{1,0:T(8,128)(2,1)S(1)}, u32[]{:S(2)}, u32[]{:S(2)}) collective-permute-start(bf16[32,5120]{1,0:T(8,128)(2,1)} %get-tuple-element.33), channel_id=1, source_target_pairs={{0,1},{1,2},{2,3},{3,4},{4,5},{5,6},{6,7},{7,8},{8,9},{9,10},{10,1... | collective-permute-start | bytes 983048 | tf_op jit(solution)/shard_map/ppermute | solution.py:23
  180.5 1.2 fusion.23
  181.7 5.2 %collective-permute-done.5 = bf16[32,5120]{1,0:T(8,128)(2,1)S(1)} collective-permute-done((bf16[32,5120]{1,0:T(8,128)(2,1)}, bf16[32,5120]{1,0:T(8,128)(2,1)S(1)}, u32[]{:S(2)}, u32[]{:S(2)}) %collective-permute-start.5) | collective-permute-done | bytes 327712 | tf_op jit(solution)/shard_map/ppermute | solution.py:23
  187.3 1.7 reshape.130
  189.0 95.8 %all_to_all.10 = bf16[64,2,7680]{2,1,0:T(2,128)(2,1)S(1)} all-to-all(bf16[64,2,7680]{2,1,0:T(2,128)(2,1)} %reshape.130), channel_id=1, replica_groups=mesh['section'=8,'dp'=64] {'dp'}, dimensions={0} | all-to-all | bytes 3932160 | tf_op jit(solution)/shard_map/all_to_all | solution.py:121
  286.0 8.4 %collective-permute-start.6 = (bf16[64,2,5120]{2,0,1:T(8,128)(2,1)S(1)}, bf16[64,2,5120]{2,0,1:T(8,128)(2,1)}, u32[]{:S(2)}, u32[]{:S(2)}) collective-permute-start(bf16[64,2,5120]{2,0,1:T(8,128)(2,1)S(1)} %copy.53), channel_id=1, source_target_pairs={{64,0},{128,64},{192,128},{256,192},{320,256},{384,320},{448,384},... | collective-permute-start | bytes 3932168 | tf_op jit(solution)/shard_map/ppermute | solution.py:29
  294.8 16.6 %collective-permute-done = s32[128]{0:T(128)S(1)} collective-permute-done((s32[128]{0:T(128)S(1)}, s32[128]{0:T(128)S(1)}, u32[]{:S(2)}, u32[]{:S(2)}) %collective-permute-start) | collective-permute-done | bytes 544 | tf_op jit(solution)/shard_map/ppermute | solution.py:29
  312.1 3.4 %fusion.1 = bf16[1,128,7680]{2,1,0:T(8,128)(2,1)} fusion(bf16[64,2,5120]{2,0,1:T(8,128)(2,1)} %collective-permute-done.6, bf16[64,2,2560]{2,0,1:T(8,128)(2,1)S(1)} %copy.52, s32[64,2]{0,1:T(2,128)S(1)} %copy.30), kind=kOutput, calls=%fused_computation.3 | convolution fusion | flops 256589824 | bytes 3932672 | tf_op jit(solution)/shard_map/kbg,bgf->kf/dot_general | solution.py:130
  (47 shorter events, 10.4 us)
Async XLA Ops:
  8.8 19.3 %copy-start.1 = (s32[1,8192]{1,0:T(1,128)S(1)}, s32[1,8192]{1,0:T(1,128)}, u32[]{:S(2)}) copy-start(s32[1,8192]{1,0:T(1,128)} %param.15) | copy-start | bytes 98308
  8.8 135.8 %all-to-all-start = ((bf16[64,2,10240]{2,1,0:T(2,128)(2,1)}), bf16[64,2,10240]{2,1,0:T(2,128)(2,1)S(1)}, u32[]{:S(2)}, u32[]{:S(2)}) async-start(bf16[64,2,10240]{2,1,0:T(2,128)(2,1)} %copy.32), calls=%async_computation | async-start | bytes 5242880 | tf_op jit(solution)/shard_map/all_to_all | solution.py:109
  145.9 13.9 %collective-permute-start.1 = (bf16[16,2,5120]{2,1,0:T(2,128)(2,1)}, bf16[16,2,5120]{2,1,0:T(2,128)(2,1)}, u32[]{:S(2)}, u32[]{:S(2)}) collective-permute-start(bf16[16,2,5120]{2,1,0:T(2,128)(2,1)} %get-tuple-element.31), channel_id=1, source_target_pairs={{0,1},{1,2},{2,3},{3,4},{4,5},{5,6},{6,7},{7,8},{8,9},{9,10},{10,1... | collective-permute-start | bytes 983048 | tf_op jit(solution)/shard_map/ppermute | solution.py:15
  154.1 10.2 %collective-permute-start.2 = (bf16[16,2,5120]{2,1,0:T(2,128)(2,1)}, bf16[16,2,5120]{2,1,0:T(2,128)(2,1)}, u32[]{:S(2)}, u32[]{:S(2)}) collective-permute-start(bf16[16,2,5120]{2,1,0:T(2,128)(2,1)} %get-tuple-element.32), channel_id=1, source_target_pairs={{1,0},{2,1},{3,2},{4,3},{5,4},{6,5},{7,6},{8,7},{9,8},{10,9},{11,1... | collective-permute-start | bytes 983048 | tf_op jit(solution)/shard_map/ppermute | solution.py:16
  159.2 6.2 %slice-start = ((bf16[128,10240]{1,0:T(8,128)(2,1)}), bf16[128,5120]{1,0:T(8,128)(2,1)S(1)}, s32[]{:S(2)}) async-start(bf16[128,10240]{1,0:T(8,128)(2,1)} %reshape.122), calls=%async_computation.2 | async-start | bytes 2621440 | tf_op jit(solution)/shard_map/concatenate | solution.py:39
  169.4 2.7 copy-start
  170.8 9.7 %collective-permute-start.4 = (bf16[32,5120]{1,0:T(8,128)(2,1)}, bf16[32,5120]{1,0:T(8,128)(2,1)}, u32[]{:S(2)}, u32[]{:S(2)}) collective-permute-start(bf16[32,5120]{1,0:T(8,128)(2,1)} %get-tuple-element.34), channel_id=1, source_target_pairs={{1,0},{2,1},{3,2},{4,3},{5,4},{6,5},{7,6},{8,7},{9,8},{10,9},{11,1... | collective-permute-start | bytes 983048 | tf_op jit(solution)/shard_map/ppermute | solution.py:23
  173.9 13.3 %collective-permute-start.3 = (bf16[128,2560]{1,0:T(8,128)(2,1)}, bf16[128,2560]{1,0:T(8,128)(2,1)S(1)}, u32[]{:S(2)}, u32[]{:S(2)}) collective-permute-start(bf16[128,2560]{1,0:T(8,128)(2,1)} %copy.41), channel_id=1, source_target_pairs={{64,0},{128,64},{192,128},{256,192},{320,256},{384,320},{448,384},... | collective-permute-start | bytes 1966088 | tf_op jit(solution)/shard_map/ppermute | solution.py:29
  176.0 10.9 %collective-permute-start.5 = (bf16[32,5120]{1,0:T(8,128)(2,1)}, bf16[32,5120]{1,0:T(8,128)(2,1)S(1)}, u32[]{:S(2)}, u32[]{:S(2)}) collective-permute-start(bf16[32,5120]{1,0:T(8,128)(2,1)} %get-tuple-element.33), channel_id=1, source_target_pairs={{0,1},{1,2},{2,3},{3,4},{4,5},{5,6},{6,7},{7,8},{8,9},{9,10},{10,1... | collective-permute-start | bytes 983048 | tf_op jit(solution)/shard_map/ppermute | solution.py:23
  285.7 8.7 %copy-start.2 = (s32[1,1,128]{2,1,0:T(1,128)S(1)}, s32[1,1,128]{2,1,0:T(1,128)}, u32[]{:S(2)}) copy-start(s32[1,1,128]{2,1,0:T(1,128)} %param.14) | copy-start | bytes 1540
  286.0 26.1 %collective-permute-start.6 = (bf16[64,2,5120]{2,0,1:T(8,128)(2,1)S(1)}, bf16[64,2,5120]{2,0,1:T(8,128)(2,1)}, u32[]{:S(2)}, u32[]{:S(2)}) collective-permute-start(bf16[64,2,5120]{2,0,1:T(8,128)(2,1)S(1)} %copy.53), channel_id=1, source_target_pairs={{64,0},{128,64},{192,128},{256,192},{320,256},{384,320},{448,384},... | collective-permute-start | bytes 3932168 | tf_op jit(solution)/shard_map/ppermute | solution.py:29
  294.4 16.9 %collective-permute-start = (s32[128]{0:T(128)S(1)}, s32[128]{0:T(128)S(1)}, u32[]{:S(2)}, u32[]{:S(2)}) collective-permute-start(s32[128]{0:T(128)S(1)} %bitcast.73), channel_id=1, source_target_pairs={{64,0},{128,64},{192,128},{256,192},{320,256},{384,320},{448,384},... | collective-permute-start | bytes 1544 | tf_op jit(solution)/shard_map/ppermute | solution.py:29
